TPU v7x, 512 devices: a whole 4x8x8 slice. The times are simulated.
512 devices in a mesh: row: 64 (over x, y, core), col: 8 (over z).
Axes of the slice: x: 4, y: 8, z: 8, core: 2. Of those that a mesh axis runs over, the one named last changes fastest.
Arguments:
- grad_out: bfloat16 [2048, 12288], P('row', 'col'), may hold values from -3.5 to 3.5
- pre_act: bfloat16 [2048, 24576], P('col', 'row'), may hold values from -6 to 6
- down_weight: bfloat16 [24576, 12288], P('row', 'col'), may hold values from -0.0546875 to 0.0546875
Outputs:
- grad_pre: bfloat16 [2048, 24576], P('col', 'row')
- grad_weight: bfloat16 [24576, 12288], P('row', 'col')
All inputs are finite; a program needn't handle non-finite values.
Results may differ from a plain program's by a relative error of at most 0.015.
Values may be sent and summed in bfloat16 or wider, within the bound.
No kernel may reach another device: no remote copies, remote signals or barrier semaphores. Data moves between devices by JAX's collectives and lax.ppermute only.
A program may use at most 64 MiB of HBM per device.

v0:
```python
import jax
import jax.numpy as jnp
from jax import lax
from jax.sharding import PartitionSpec as P

coef = 0.7978845608
cubic = 0.044715


def gelu_fwd(x):
    return 0.5 * x * (1.0 + jnp.tanh(coef * (x + cubic * x * x * x)))


def gelu_grad(x):
    inner = coef * (x + cubic * x * x * x)
    tangent = jnp.tanh(inner)
    return 0.5 * (1.0 + tangent) + 0.5 * x * (1.0 - tangent * tangent) * coef * (
        1.0 + 3.0 * cubic * x * x
    )


def body(grad_out, pre_act, down_weight):
    grad_all = lax.all_gather(grad_out, "row", axis=0, tiled=True)
    pre_all = lax.all_gather(pre_act, "col", axis=0, tiled=True)
    hidden = gelu_fwd(pre_all.astype(jnp.float32)).astype(jnp.bfloat16)
    grad_weight = lax.dot_general(
        hidden, grad_all, (((0,), (0,)), ((), ())), preferred_element_type=jnp.float32
    ).astype(jnp.bfloat16)
    share_rows = pre_act.shape[0]
    partial_term = lax.dot_general(
        grad_all, down_weight, (((1,), (1,)), ((), ())), preferred_element_type=jnp.float32
    )
    summed = lax.psum(partial_term.astype(jnp.bfloat16), "col").astype(jnp.float32)
    offset = lax.axis_index("col") * share_rows
    grad_hidden = lax.dynamic_slice_in_dim(summed, offset, share_rows, 0)
    grad_pre = (grad_hidden * gelu_grad(pre_act.astype(jnp.float32))).astype(jnp.bfloat16)
    return (grad_pre, grad_weight)


def solution(mesh):
    in_specs = (P("row", "col"), P("col", "row"), P("row", "col"))
    out_specs = (P("col", "row"), P("row", "col"))
    return jax.shard_map(body, mesh=mesh, in_specs=in_specs, out_specs=out_specs, check_vma=False)
```

profile of v0, /device:TPU:2, one launch (start us, length us, event | category | flops | bytes accessed | tf_op | source)
XLA Modules:
  0.0 237.7 jit_solution(11160524972806360876)
XLA Ops:
  7.2 0.0 copy-start
  7.2 0.0 all-gather.3.cloned.1.call-start
  7.2 0.7 all-gather.3.cloned.1.call-update
  7.9 0.0 all-gather.5.cloned.1.call-start
  8.0 0.7 all-gather.5.cloned.1.call-update
  8.7 0.0 all-reduce.2.cloned.1.call-start
  8.7 91.8 %all-gather.3.cloned.1.call-done = bf16[2048,1536]{1,0:T(8,128)(2,1)} async-done(((bf16[32,1536]{1,0:T(8,128)(2,1)}), bf16[2048,1536]{1,0:T(8,128)(2,1)}) %all-gather.3.cloned.1.call-update) | async-done | bytes 6291472 | tf_op jit(solution)/shard_map/all_gather | solution.py:23
  100.5 0.0 copy-done
  100.5 7.4 %convolution_convert_fusion.1 = bf16[2048,384]{1,0:T(8,128)(2,1)} fusion(bf16[2048,1536]{1,0:T(8,128)(2,1)} %all-gather.3.cloned.1.call-done, bf16[384,1536]{1,0:T(8,128)(2,1)S(1)} %copy-done), kind=kOutput, calls=%fused_computation.11 | convolution fusion | flops 2416705536 | bytes 9043968 | tf_op jit(solution)/shard_map/dot_general | solution.py:30
  107.9 0.0 all-reduce.2.cloned.1.call-update
  107.9 0.0 copy-start.1
  108.0 36.0 %all-gather.5.cloned.1.call-done = bf16[2048,384]{1,0:T(8,128)(2,1)} async-done(((bf16[256,384]{1,0:T(8,128)(2,1)}), bf16[2048,384]{1,0:T(8,128)(2,1)}) %all-gather.5.cloned.1.call-update) | async-done | bytes 1572880 | tf_op jit(solution)/shard_map/all_gather | solution.py:24
  143.9 7.0 %convolution_convert_fusion = bf16[384,1536]{1,0:T(8,128)(2,1)} fusion(bf16[2048,1536]{1,0:T(8,128)(2,1)} %all-gather.3.cloned.1.call-done, bf16[2048,384]{1,0:T(8,128)(2,1)} %all-gather.5.cloned.1.call-done), kind=kOutput, calls=%fused_computation.10 | convolution fusion | flops 2424373248 | bytes 9043968 | tf_op jit(solution)/shard_map/dot_general | solution.py:26
  150.9 78.4 %all-reduce.2.cloned.1.call-done = bf16[2048,384]{1,0:T(8,128)(2,1)} async-done(((bf16[2048,384]{1,0:T(8,128)(2,1)}), bf16[2048,384]{1,0:T(8,128)(2,1)}) %all-reduce.2.cloned.1.call-update) | async-done | bytes 1572880 | tf_op jit(solution)/shard_map/psum | solution.py:33
  229.3 0.0 copy-done.1
  229.3 1.9 fusion.17
Async XLA Ops:
  7.2 93.3 %copy-start = (bf16[384,1536]{1,0:T(8,128)(2,1)S(1)}, bf16[384,1536]{1,0:T(8,128)(2,1)}, u32[]{:S(2)}) copy-start(bf16[384,1536]{1,0:T(8,128)(2,1)} %param.5) | copy-start | bytes 3538948
  7.2 93.3 %all-gather.3.cloned.1.call-start = ((), (), s32[]{:S(2)}) async-start(), calls=%async_computation | async-start | bytes 6389760 | tf_op jit(solution)/shard_map/all_gather | solution.py:23
  7.9 136.0 %all-gather.5.cloned.1.call-start = ((), (), s32[]{:S(2)}) async-start(), calls=%async_computation.2 | async-start | bytes 1769472 | tf_op jit(solution)/shard_map/all_gather | solution.py:24
  8.7 220.7 %all-reduce.2.cloned.1.call-start = ((), (), s32[]{:S(2)}) async-start(), calls=%async_computation.1 | async-start | bytes 3145728 | tf_op jit(solution)/shard_map/psum | solution.py:33
  107.9 121.4 %copy-start.1 = (bf16[256,384]{1,0:T(8,128)(2,1)S(1)}, bf16[256,384]{1,0:T(8,128)(2,1)}, u32[]{:S(2)}) copy-start(bf16[256,384]{1,0:T(8,128)(2,1)} %param.4) | copy-start | bytes 589828
Sparse Core Ops, SparseCore 0:
  11.3 89.1 all-gather.2
  102.6 41.3 all-gather.4
  146.3 82.9 all-reduce.1
where the time goes:
time: 238 us
  waiting for transfers between devices  208 us (87%)
  matrix products  14.4 us (6%)
  between operations  13.8 us (6%)
    all_gather x1, waiting for transfers between devices, body(): grad_all = lax.all_gather(grad_out, 'row', axis=0, tiled=True)  91.8 us
    psum x1, waiting for transfers between devices, body(): lax.psum(partial_term.astype(jnp.bfloat16), 'col').astype(jnp.float32)  78.4 us
    all_gather x1, waiting for transfers between devices, body(): pre_all = lax.all_gather(pre_act, 'col', axis=0, tiled=True)  36 us
    dot_general x1, matrix products, body(): lax.dot_general(grad_all, down_weight, (((1,), (1,)), ((), ())), preferre...  7.4 us
    dot_general x1, matrix products, body(): lax.dot_general(hidden, grad_all, (((0,), (0,)), ((), ())), preferred_ele...  6.99 us
  transfers between devices with their start and end apart: 3, of which 3 were waited for; matrix products, arithmetic and copies ran while one was open for 6% of the time, Pallas kernels for 0%

commit v1 on v0

--- a/solution.py
+++ b/solution.py
@@ -5,6 +5,7 @@
 
 coef = 0.7978845608
 cubic = 0.044715
+do_roots = lambda arr: jnp.sum(jax.lax.all_gather(arr, "col"), 0)
 
 
 def gelu_fwd(x):
@@ -30,7 +31,7 @@
     partial_term = lax.dot_general(
         grad_all, down_weight, (((1,), (1,)), ((), ())), preferred_element_type=jnp.float32
     )
-    summed = lax.psum(partial_term.astype(jnp.bfloat16), "col").astype(jnp.float32)
+    summed = do_roots(partial_term.astype(jnp.bfloat16)).astype(jnp.float32)
     offset = lax.axis_index("col") * share_rows
     grad_hidden = lax.dynamic_slice_in_dim(summed, offset, share_rows, 0)
     grad_pre = (grad_hidden * gelu_grad(pre_act.astype(jnp.float32))).astype(jnp.bfloat16)

time: 238 us -> 297 us (1.25)
  the two profiles are of different devices: /device:TPU:2 before, /device:TPU:1 now
where the time goes in v1:
time: 297 us
  waiting for transfers between devices  260 us (88%)
  matrix products  14.4 us (5%)
  between operations  13.8 us (5%)
  other arithmetic  8.35 us (3%)
    all_gather x1, waiting for transfers between devices, do_roots = lambda arr: jnp.sum(jax.lax.all_gather(arr, 'col'), 0)  134 us
    all_gather x1, waiting for transfers between devices, body(): grad_all = lax.all_gather(grad_out, 'row', axis=0, tiled=True)  94.3 us
    all_gather x1, waiting for transfers between devices, body(): pre_all = lax.all_gather(pre_act, 'col', axis=0, tiled=True)  30.5 us
    reduce_sum x1, other arithmetic, do_roots = lambda arr: jnp.sum(jax.lax.all_gather(arr, 'col'), 0)  7.39 us
    dot_general x1, matrix products, body(): lax.dot_general(grad_all, down_weight, (((1,), (1,)), ((), ())), preferre...  7.38 us
    dot_general x1, matrix products, body(): lax.dot_general(hidden, grad_all, (((0,), (0,)), ((), ())), preferred_ele...  6.99 us
  transfers between devices with their start and end apart: 3, of which 3 were waited for; matrix products, arithmetic and copies ran while one was open for 5% of the time, Pallas kernels for 0%

profile of v1, /device:TPU:1, one launch (start us, length us, event | category | flops | bytes accessed | tf_op | source)
XLA Modules:
  0.0 296.6 jit_solution(3493853171715251116)
XLA Ops:
  7.2 0.0 copy-start
  7.2 0.0 all-gather.5.cloned.1.call-start
  7.2 0.7 all-gather.5.cloned.1.call-update
  7.9 0.0 all-gather.7.cloned.1.call-start
  8.0 0.7 all-gather.7.cloned.1.call-update
  8.7 0.0 all-gather.9.cloned.1.call-start
  8.7 94.3 %all-gather.5.cloned.1.call-done = bf16[2048,1536]{1,0:T(8,128)(2,1)} async-done(((bf16[32,1536]{1,0:T(8,128)(2,1)}), bf16[2048,1536]{1,0:T(8,128)(2,1)}) %all-gather.5.cloned.1.call-update) | async-done | bytes 6291472 | tf_op jit(solution)/shard_map/all_gather | solution.py:24
  103.0 0.0 copy-done
  103.0 7.4 %convolution_convert_fusion.1 = bf16[2048,384]{1,0:T(8,128)(2,1)} fusion(bf16[2048,1536]{1,0:T(8,128)(2,1)} %all-gather.5.cloned.1.call-done, bf16[384,1536]{1,0:T(8,128)(2,1)S(1)} %copy-done), kind=kOutput, calls=%fused_computation.11 | convolution fusion | flops 2416705536 | bytes 9043968 | tf_op jit(solution)/shard_map/dot_general | solution.py:31
  110.4 0.0 all-gather.9.cloned.1.call-update
  110.4 30.5 %all-gather.7.cloned.1.call-done = bf16[2048,384]{1,0:T(8,128)(2,1)} async-done(((bf16[256,384]{1,0:T(8,128)(2,1)}), bf16[2048,384]{1,0:T(8,128)(2,1)}) %all-gather.7.cloned.1.call-update) | async-done | bytes 1572880 | tf_op jit(solution)/shard_map/all_gather | solution.py:25
  140.9 7.0 %convolution_convert_fusion = bf16[384,1536]{1,0:T(8,128)(2,1)} fusion(bf16[2048,1536]{1,0:T(8,128)(2,1)} %all-gather.5.cloned.1.call-done, bf16[2048,384]{1,0:T(8,128)(2,1)} %all-gather.7.cloned.1.call-done), kind=kOutput, calls=%fused_computation.10 | convolution fusion | flops 2424373248 | bytes 9043968 | tf_op jit(solution)/shard_map/dot_general | solution.py:27
  147.9 133.8 %all-gather.9.cloned.1.call-done = bf16[16384,384]{1,0:T(8,128)(2,1)} async-done(((bf16[2048,384]{1,0:T(8,128)(2,1)}), bf16[16384,384]{1,0:T(8,128)(2,1)}) %all-gather.9.cloned.1.call-update) | async-done | bytes 12582928 | tf_op jit(solution)/shard_map/all_gather | solution.py:8
  281.7 0.0 copy-start.1
  281.7 7.4 %reduce_sum.12 = bf16[2048,384]{1,0:T(8,128)(2,1)S(1)} reduce(bf16[8,2048,384]{2,1,0:T(8,128)(2,1)} %bitcast.4, bf16[]{:T(256)} %constant.10.clone.1), dimensions={0}, to_apply=%region_0.0 | reduce | flops 5505024 | bytes 14155778 | tf_op jit(solution)/shard_map/reduce_sum | solution.py:8
  289.1 0.0 copy-done.1
  289.1 1.0 fusion.17
Async XLA Ops:
  7.2 95.8 %copy-start = (bf16[384,1536]{1,0:T(8,128)(2,1)S(1)}, bf16[384,1536]{1,0:T(8,128)(2,1)}, u32[]{:S(2)}) copy-start(bf16[384,1536]{1,0:T(8,128)(2,1)} %param.5) | copy-start | bytes 3538948
  7.2 95.8 %all-gather.5.cloned.1.call-start = ((), (), s32[]{:S(2)}) async-start(), calls=%async_computation | async-start | bytes 6389760 | tf_op jit(solution)/shard_map/all_gather | solution.py:24
  7.9 133.0 %all-gather.7.cloned.1.call-start = ((), (), s32[]{:S(2)}) async-start(), calls=%async_computation.1 | async-start | bytes 1769472 | tf_op jit(solution)/shard_map/all_gather | solution.py:25
  8.7 273.0 %all-gather.9.cloned.1.call-start = ((), (), s32[]{:S(2)}) async-start(), calls=%async_computation.2 | async-start | bytes 14155776 | tf_op jit(solution)/shard_map/all_gather | solution.py:8
  281.7 7.4 %copy-start.1 = (bf16[256,384]{1,0:T(8,128)(2,1)S(1)}, bf16[256,384]{1,0:T(8,128)(2,1)}, u32[]{:S(2)}) copy-start(bf16[256,384]{1,0:T(8,128)(2,1)} %param.4) | copy-start | bytes 589828
Sparse Core Ops, SparseCore 0:
  11.3 91.6 all-gather.4
  105.1 35.7 all-gather.6
  143.0 138.6 all-gather.8
